TPU v7x, 256 devices: a whole 4x4x8 slice. The times are simulated.
256 devices in a mesh: user: 16 (over y, z_hi, core), party: 16 (over x, z_lo).
Axes of the slice: x: 4, y: 4, z: 8 (z_hi: 2, z_lo: 4; z = z_hi * 4 + z_lo), core: 2. Of those that a mesh axis runs over, the one named last changes fastest.
Arguments:
- ratings: bfloat16 [1024, 16384], P('party', 'user'), may hold values from -6 to 6
- rating_mask: int32 [1024, 16384], P('party', 'user'), may hold values 0 or 1
- user_factors: bfloat16 [16384, 256], P('user'), may hold values from -0.375 to 0.375
- item_factors: bfloat16 [1024, 256], replicated, may hold values from -6 to 6
- item_index: int32 [1024], replicated, may hold values from 0 to 1023, each once
- features: bfloat16 [1024, 524288], P(None, ('user', 'party')), may hold values from -6 to 6
- ridge_weights: bfloat16 [524288, 256], P(('user', 'party')), may hold values from -10 to 10
Outputs:
- new_factors: float32 [1024, 256], P('party')
- fitted_weights: float32 [524288, 256], P(('user', 'party'))
Inputs may be any that keep to these rules, and one draw needn't show every extreme that they name: `item_index`: each window item stands at exactly one tile position.
All inputs are finite; a program needn't handle non-finite values. No bound on the sum of `rating_mask` on one device may be relied on, other than what follows from the above.
Results may differ from a plain program's by a relative error of at most 0.00032.
Values may be sent and summed in bfloat16 or wider, within the bound.
No kernel may reach another device: no remote copies, remote signals or barrier semaphores. Data moves between devices by JAX's collectives and lax.ppermute only.
A program may use at most 64 MiB of HBM per device.

v0:
```python
import jax
import jax.numpy as jnp
from jax import lax
from jax.experimental import pallas as pl
from jax.experimental.pallas import tpu as pltpu
from jax.sharding import PartitionSpec as P

ITERS = 2


learn_rate = 0.05
factor_decay = 1.0
ridge_decay = 0.05
ridge_step = 0.05

ALL = ("user", "party")


def reduce_scatter_tiles(x, n):
    rows, cols = x.shape
    tiles = x.reshape(rows // 8, 8, cols // 128, 128).transpose(0, 2, 1, 3).reshape(n, 8, 128)
    return lax.all_to_all(tiles, ALL, 0, 0, tiled=True).sum(0)


def gather_tiles(block, n, shape):
    rows, cols = shape
    sent = jnp.broadcast_to(block[None], (n,) + block.shape)
    got = lax.all_to_all(sent, ALL, 0, 0, tiled=True)
    return got.reshape(rows // 8, cols // 128, 8, 128).transpose(0, 2, 1, 3).reshape(rows, cols)


def total_scalar(value, n):
    sent = jnp.broadcast_to(value, (n, 1, 128))
    return lax.all_to_all(sent, ALL, 0, 0, tiled=True).sum(0)[0, 0]


def final_kernel(scale_ref, w_ref, *refs):
    *grad_refs, out_ref = refs
    w = w_ref[...].astype(jnp.float32)
    for k, grad_ref in enumerate(grad_refs):
        w = w - ridge_step * grad_ref[...].T * scale_ref[k]
    out_ref[...] = w


def final_weights(ridge_weights, grads, scales, block=1024):
    rows, cols = ridge_weights.shape
    grad_spec = pl.BlockSpec((cols, block), lambda i: (0, i))
    row_spec = pl.BlockSpec((block, cols), lambda i: (i, 0))
    return pl.pallas_call(
        final_kernel,
        grid=(rows // block,),
        in_specs=[pl.BlockSpec(memory_space=pltpu.SMEM), row_spec] + [grad_spec] * len(grads),
        out_specs=row_spec,
        out_shape=jax.ShapeDtypeStruct((rows, cols), jnp.float32),
    )(jnp.stack(scales), ridge_weights, *[g.T for g in grads])


def body(ratings, rating_mask, user_factors, item_factors, item_index, features, ridge_weights):
    local_items = ratings.shape[0]
    party_pos = lax.axis_index("party")
    user_pos = lax.axis_index("user")
    devices_all = lax.axis_size(ALL)
    local_index = lax.dynamic_slice_in_dim(item_index, party_pos * local_items, local_items)
    tile_rows = jnp.take(item_factors, local_index, axis=0)
    scores = lax.dot_general(
        tile_rows, user_factors, (((1,), (1,)), ((), ())), preferred_element_type=jnp.float32
    )
    misfit = (rating_mask.astype(jnp.float32) * (scores - ratings.astype(jnp.float32))).astype(
        jnp.bfloat16
    )
    partial_grad = jnp.dot(misfit, user_factors, preferred_element_type=jnp.float32)
    grad_total = lax.psum(partial_grad, "user")
    tile_wide = tile_rows.astype(jnp.float32)
    new_factors = tile_wide - learn_rate * (grad_total + factor_decay * tile_wide)
    own_tile = jnp.where(user_pos == 0, tile_wide - learn_rate * factor_decay * tile_wide, 0.0)
    share = learn_rate * partial_grad - own_tile
    items = item_factors.shape[0]
    minus_targets = jnp.zeros((items, share.shape[1]), jnp.float32).at[local_index].set(share)
    total_features = features.shape[1] * devices_all
    feature_scale = 1.0 / float(total_features) ** 0.5
    weights = ridge_weights.astype(jnp.float32)
    grads, scales = [], []
    for iteration in range(ITERS):
        weights_bf = weights.astype(jnp.bfloat16)
        partial_pred = (
            jnp.dot(features, weights_bf, preferred_element_type=jnp.float32) * feature_scale
        )
        error_block = reduce_scatter_tiles(partial_pred + minus_targets, devices_all)
        error_rows = gather_tiles(error_block.astype(jnp.bfloat16), devices_all, partial_pred.shape)
        grad = (
            lax.dot_general(
                features, error_rows, (((0,), (0,)), ((), ())), preferred_element_type=jnp.float32
            )
            * feature_scale
            + ridge_decay * weights
        )
        total_sq = total_scalar(jnp.sum(grad * grad), devices_all)
        mean_sq = total_sq / float(total_features * grad.shape[1])
        scale = lax.rsqrt(mean_sq + 1e-06)
        grads.append(grad)
        scales.append(scale)
        if iteration < ITERS - 1:
            weights = weights - ridge_step * grad * scale
    return (new_factors, final_weights(ridge_weights, grads, scales))


def solution(mesh):
    in_specs = (
        P("party", "user"),
        P("party", "user"),
        P("user", None),
        P(),
        P(),
        P(None, ALL),
        P(ALL, None),
    )
    out_specs = (P("party", None), P(ALL, None))
    return jax.shard_map(body, mesh=mesh, in_specs=in_specs, out_specs=out_specs, check_vma=False)
```

profile of v0, /device:TPU:1, one launch (start us, length us, event | category | flops | bytes accessed | tf_op | source)
XLA Modules:
  0.0 349.3 jit_solution(2351018616481977567)
XLA Ops:
  7.2 0.9 compare_and_fusion
  8.2 0.7 gather_fusion
  8.9 1.8 fusion.10
  10.8 1.1 scatter_custom_fusion
  11.9 3.8 %fusion.6 = f32[1024,256]{1,0:T(8,128)S(1)} fusion(f32[1024,256]{1,0:T(8,128)S(1)} %scatter_custom_fusion, bf16[1024,2048]{1,0:T(8,128)(2,1)} %param.12, bf16[2048,256]{1,0:T(8,128)(2,1)S(1)} %copy-done.3), kind=kOutput, calls=%fused_computation.16 | convolution fusion | flops 1074266112 | bytes 7340032 | tf_op jit(solution)/shard_map/dot_general | solution.py:86
  15.8 47.4 %all_to_all.30 = f32[256,8,128]{2,1,0:T(8,128)S(1)} all-to-all(f32[256,8,128]{2,1,0:T(8,128)S(1)} %bitcast.58), channel_id=1, replica_groups=mesh['user'=16,'party'=16] {'user','party'}, dimensions={0} | all-to-all | bytes 2097152 | tf_op jit(solution)/shard_map/all_to_all | solution.py:22
  63.5 0.9 broadcast_in_dim.43
  64.4 5.1 %all-to-all-start.1 = ((bf16[256,8,128]{2,1,0:T(8,128)(2,1)}), bf16[256,8,128]{2,1,0:T(8,128)(2,1)S(1)}, u32[]{:S(2)}, u32[]{:S(2)}) async-start(bf16[256,8,128]{2,1,0:T(8,128)(2,1)} %broadcast_in_dim.43), calls=%async_computation.1 | async-start | bytes 1048576 | tf_op jit(solution)/shard_map/all_to_all | solution.py:28
  69.5 1.4 copy.13
  70.9 19.7 %all-to-all-done.1 = bf16[256,8,128]{2,1,0:T(8,128)(2,1)S(1)} async-done(((bf16[256,8,128]{2,1,0:T(8,128)(2,1)}), bf16[256,8,128]{2,1,0:T(8,128)(2,1)S(1)}, u32[]{:S(2)}, u32[]{:S(2)}) %all-to-all-start.1) | async-done | bytes 524320 | tf_op jit(solution)/shard_map/all_to_all | solution.py:28
  90.7 4.6 %multiply_reduce_fusion.1 = (f32[]{:T(128)}, f32[2048,256]{0,1:T(8,128)S(1)}) fusion(bf16[2048,256]{0,1:T(8,128)(2,1)} %copy.13, bf16[1024,256]{1,0:T(8,128)(2,1)S(1)} %bitcast.56, bf16[1024,2048]{1,0:T(8,128)(2,1)} %param.12), kind=kOutput, calls=%fused_computation.11 | convolution fusion | flops 1076887552 | bytes 7864324 | tf_op jit(solution)/shard_map/dot_general | solution.py:91
  95.9 18.1 %all_to_all.31 = f32[256,1,128]{2,1,0:T(1,128)S(1)} all-to-all(f32[256,1,128]{2,1,0:T(1,128)S(1)} %broadcast_in_dim.44), channel_id=1, replica_groups=mesh['user'=16,'party'=16] {'user','party'}, dimensions={0} | all-to-all | bytes 262144 | tf_op jit(solution)/shard_map/all_to_all | solution.py:34
  114.2 4.1 %fusion.7 = f32[1024,256]{1,0:T(8,128)S(1)} fusion(f32[1024,256]{1,0:T(8,128)} %copy-done.2, bf16[1024,2048]{1,0:T(8,128)(2,1)} %param.12, f32[2048,256]{0,1:T(8,128)S(1)} %get-tuple-element.5, bf16[2048,256]{0,1:T(8,128)(2,1)} %copy.13, f32[]{:T(128)} %bitcast.10), kind=kOutput, calls=%fused_computation.17 | convolution fusion | flops 1076363264 | bytes 9437188 | tf_op jit(solution)/shard_map/dot_general | solution.py:86
  118.3 38.5 %all_to_all.32 = f32[256,8,128]{2,1,0:T(8,128)} all-to-all(f32[256,8,128]{2,1,0:T(8,128)S(1)} %bitcast.55), channel_id=1, replica_groups=mesh['user'=16,'party'=16] {'user','party'}, dimensions={0} | all-to-all | bytes 2097152 | tf_op jit(solution)/shard_map/all_to_all | solution.py:22
  156.8 1.5 reduce_sum.62
  158.3 0.9 broadcast_in_dim.45
  159.2 5.3 %all-to-all-start.4 = ((bf16[256,8,128]{2,1,0:T(8,128)(2,1)}), bf16[256,8,128]{2,1,0:T(8,128)(2,1)S(1)}, u32[]{:S(2)}, u32[]{:S(2)}) async-start(bf16[256,8,128]{2,1,0:T(8,128)(2,1)} %broadcast_in_dim.45), calls=%async_computation.4 | async-start | bytes 1048576 | tf_op jit(solution)/shard_map/all_to_all | solution.py:28
  165.3 20.2 %all-to-all-done.4 = bf16[256,8,128]{2,1,0:T(8,128)(2,1)S(1)} async-done(((bf16[256,8,128]{2,1,0:T(8,128)(2,1)}), bf16[256,8,128]{2,1,0:T(8,128)(2,1)S(1)}, u32[]{:S(2)}, u32[]{:S(2)}) %all-to-all-start.4) | async-done | bytes 524320 | tf_op jit(solution)/shard_map/all_to_all | solution.py:28
  185.5 5.9 %multiply_reduce_fusion = (f32[]{:T(128)}, f32[2048,256]{0,1:T(8,128)}) fusion(f32[2048,256]{0,1:T(8,128)S(1)} %get-tuple-element.5, f32[]{:T(128)} %bitcast.10, bf16[2048,256]{0,1:T(8,128)(2,1)} %copy.13, bf16[1024,256]{1,0:T(8,128)(2,1)S(1)} %bitcast.57, bf16[1024,2048]{1,0:T(8,128)(2,1)} %param.12), kind=kOutput, calls=%fused_computation.10 | convolution fusion | flops 1077936128 | bytes 9961480 | tf_op jit(solution)/shard_map/dot_general | solution.py:91
  191.4 1.3 broadcast_in_dim.46
  192.8 5.5 %all-to-all-start.5 = ((f32[256,1,128]{2,1,0:T(1,128)}), f32[256,1,128]{2,1,0:T(1,128)S(1)}, u32[]{:S(2)}, u32[]{:S(2)}) async-start(f32[256,1,128]{2,1,0:T(1,128)} %broadcast_in_dim.46), calls=%async_computation.5 | async-start | bytes 262144 | tf_op jit(solution)/shard_map/all_to_all | solution.py:34
  198.3 137.8 %all-reduce.2.cloned.1.call-done = f32[64,256]{1,0:T(8,128)} async-done(((f32[64,256]{1,0:T(8,128)}), f32[64,256]{1,0:T(8,128)}) %all-reduce.2.cloned.1.call-update) | async-done | bytes 65552 | tf_op jit(solution)/shard_map/psum | solution.py:72
  336.1 1.5 convert_subtract_fusion.2
  338.4 4.1 %shard_map.86 = f32[2048,256]{1,0:T(8,128)} custom-call(f32[2]{0:T(128)} %pad_maximum_fusion.scale_ref, bf16[2048,256]{1,0:T(8,128)(2,1)} %w_ref.1, f32[256,2048]{1,0:T(8,128)} %bitcast.53, f32[256,2048]{1,0:T(8,128)} %bitcast.54), custom_call_target="tpu_custom_call" | custom-call | tf_op jit(solution)/shard_map/pallas_call | solution.py:49
  (19 shorter events, 2.5 us)
Async XLA Ops:
  7.2 1.1 copy-start
  7.2 4.7 %copy-start.3 = (bf16[2048,256]{1,0:T(8,128)(2,1)S(1)}, bf16[2048,256]{1,0:T(8,128)(2,1)}, u32[]{:S(2)}) copy-start(bf16[2048,256]{1,0:T(8,128)(2,1)} %w_ref.1) | copy-start | bytes 3145732
  10.8 5.0 %copy-start.4 = (f32[64,256]{1,0:T(8,128)}, f32[64,256]{1,0:T(8,128)S(1)}, u32[]{:S(2)}) copy-start(f32[64,256]{1,0:T(8,128)S(1)} %fusion.10) | copy-start | bytes 196612
  11.9 3.9 %copy-start.2 = (f32[1024,256]{1,0:T(8,128)}, f32[1024,256]{1,0:T(8,128)S(1)}, u32[]{:S(2)}) copy-start(f32[1024,256]{1,0:T(8,128)S(1)} %scatter_custom_fusion) | copy-start | bytes 3145732
  64.4 26.3 %all-to-all-start.1 = ((bf16[256,8,128]{2,1,0:T(8,128)(2,1)}), bf16[256,8,128]{2,1,0:T(8,128)(2,1)S(1)}, u32[]{:S(2)}, u32[]{:S(2)}) async-start(bf16[256,8,128]{2,1,0:T(8,128)(2,1)} %broadcast_in_dim.43), calls=%async_computation.1 | async-start | bytes 1048576 | tf_op jit(solution)/shard_map/all_to_all | solution.py:28
  95.3 90.2 %copy-start.1 = (f32[2048,256]{0,1:T(8,128)}, f32[2048,256]{0,1:T(8,128)S(1)}, u32[]{:S(2)}) copy-start(f32[2048,256]{0,1:T(8,128)S(1)} %get-tuple-element.5) | copy-start | bytes 6291460
  159.2 26.3 %all-to-all-start.4 = ((bf16[256,8,128]{2,1,0:T(8,128)(2,1)}), bf16[256,8,128]{2,1,0:T(8,128)(2,1)S(1)}, u32[]{:S(2)}, u32[]{:S(2)}) async-start(bf16[256,8,128]{2,1,0:T(8,128)(2,1)} %broadcast_in_dim.45), calls=%async_computation.4 | async-start | bytes 1048576 | tf_op jit(solution)/shard_map/all_to_all | solution.py:28
  164.6 171.5 %all-reduce.2.cloned.1.call-start = ((), (), s32[]{:S(2)}) async-start(), calls=%async_computation.6 | async-start | bytes 131072 | tf_op jit(solution)/shard_map/psum | solution.py:72
  192.8 144.9 %all-to-all-start.5 = ((f32[256,1,128]{2,1,0:T(1,128)}), f32[256,1,128]{2,1,0:T(1,128)S(1)}, u32[]{:S(2)}, u32[]{:S(2)}) async-start(f32[256,1,128]{2,1,0:T(1,128)} %broadcast_in_dim.46), calls=%async_computation.5 | async-start | bytes 262144 | tf_op jit(solution)/shard_map/all_to_all | solution.py:34
Sparse Core Ops, SparseCore 0:
  168.6 167.4 all-reduce.1
where the time goes:
time: 350 us; the launch traced here: 349 us
  waiting for transfers between devices  178 us (51%)
  blocking collectives  104 us (30%)
  matrix products  20.3 us (6%)
  starting transfers between devices  16.1 us (5%)
  between operations  14.3 us (4%)
  other arithmetic  6.04 us (2%)
  local copies, waits for them, and re-layouts  5.95 us (2%)
  Pallas kernels  4.08 us (1%)
    psum x1, waiting for transfers between devices, body(): grad_total = lax.psum(partial_grad, 'user')  138 us
    all_to_all x2, blocking collectives, reduce_scatter_tiles(): return lax.all_to_all(tiles, ALL, 0, 0, tiled=True).sum(0)  86 us
    all_to_all x2, waiting for transfers between devices, gather_tiles(): got = lax.all_to_all(sent, ALL, 0, 0, tiled=True)  40 us
    all_to_all x1, blocking collectives, total_scalar(): return lax.all_to_all(sent, ALL, 0, 0, tiled=True).sum(0)[0, 0]  18.1 us
    dot_general x2, matrix products, body(): lax.dot_general(features, error_rows, (((0,), (0,)), ((), ())), preferred...  10.6 us
    all_to_all x2, starting transfers between devices, gather_tiles(): got = lax.all_to_all(sent, ALL, 0, 0, tiled=True)  10.5 us
    dot_general x2, matrix products, body(): jnp.dot(features, weights_bf, preferred_element_type=jnp.float32)  7.91 us
  transfers between devices with their start and end apart: 4, of which 3 were waited for; matrix products, arithmetic and copies ran while one was open for 3% of the time, Pallas kernels for 0%

commit v1 on v0

--- a/solution.py
+++ b/solution.py
@@ -34,25 +34,24 @@
     return lax.all_to_all(sent, ALL, 0, 0, tiled=True).sum(0)[0, 0]
 
 
-def final_kernel(scale_ref, w_ref, *refs):
-    *grad_refs, out_ref = refs
+def ahead_kernel(scale_ref, w_ref, first_ref, last_ref, w_out_ref, last_out_ref):
     w = w_ref[...].astype(jnp.float32)
-    for k, grad_ref in enumerate(grad_refs):
-        w = w - ridge_step * grad_ref[...].T * scale_ref[k]
-    out_ref[...] = w
+    w_out_ref[...] = w - ridge_step * first_ref[...].T * scale_ref[0]
+    last_out_ref[...] = last_ref[...].T
 
 
-def final_weights(ridge_weights, grads, scales, block=1024):
+def step_ahead(ridge_weights, first, scale, last, block=1024):
     rows, cols = ridge_weights.shape
     grad_spec = pl.BlockSpec((cols, block), lambda i: (0, i))
     row_spec = pl.BlockSpec((block, cols), lambda i: (i, 0))
+    shape = jax.ShapeDtypeStruct((rows, cols), jnp.float32)
     return pl.pallas_call(
-        final_kernel,
+        ahead_kernel,
         grid=(rows // block,),
-        in_specs=[pl.BlockSpec(memory_space=pltpu.SMEM), row_spec] + [grad_spec] * len(grads),
-        out_specs=row_spec,
-        out_shape=jax.ShapeDtypeStruct((rows, cols), jnp.float32),
-    )(jnp.stack(scales), ridge_weights, *[g.T for g in grads])
+        in_specs=[pl.BlockSpec(memory_space=pltpu.SMEM), row_spec, grad_spec, grad_spec],
+        out_specs=[row_spec, row_spec],
+        out_shape=[shape, shape],
+    )(scale.reshape(1), ridge_weights, first.T, last.T)
 
 
 def body(ratings, rating_mask, user_factors, item_factors, item_index, features, ridge_weights):
@@ -101,7 +100,8 @@
         scales.append(scale)
         if iteration < ITERS - 1:
             weights = weights - ridge_step * grad * scale
-    return (new_factors, final_weights(ridge_weights, grads, scales))
+    stepped, last = step_ahead(ridge_weights, grads[0], scales[0], grads[1])
+    return (new_factors, stepped - ridge_step * last * scales[1])
 
 
 def solution(mesh):

time: 350 us -> 354 us (1.011)
    sub x0 -> x1, other arithmetic: none -> 3.81 us  [body(): return (new_factors, stepped - ridge_step * last * scales[1])]
  transfers between devices with their start and end apart: 4 -> 4, of which waited for: 3 -> 3; matrix products, arithmetic and copies ran while one was open for 3% -> 3% of each run, Pallas kernels for 0% -> 1%
where the time goes in v1:
time: 354 us; the launch traced here: 353 us
  waiting for transfers between devices  178 us (50%)
  blocking collectives  104 us (29%)
  matrix products  20.5 us (6%)
  starting transfers between devices  16 us (5%)
  between operations  14.3 us (4%)
  other arithmetic  9.26 us (3%)
  local copies, waits for them, and re-layouts  6.17 us (2%)
  Pallas kernels  4.16 us (1%)
    psum x1, waiting for transfers between devices, body(): grad_total = lax.psum(partial_grad, 'user')  138 us
    all_to_all x2, blocking collectives, reduce_scatter_tiles(): return lax.all_to_all(tiles, ALL, 0, 0, tiled=True).sum(0)  86 us
    all_to_all x2, waiting for transfers between devices, gather_tiles(): got = lax.all_to_all(sent, ALL, 0, 0, tiled=True)  39.9 us
    all_to_all x1, blocking collectives, total_scalar(): return lax.all_to_all(sent, ALL, 0, 0, tiled=True).sum(0)[0, 0]  18.1 us
    dot_general x2, matrix products, body(): lax.dot_general(features, error_rows, (((0,), (0,)), ((), ())), preferred...  10.8 us
    all_to_all x2, starting transfers between devices, gather_tiles(): got = lax.all_to_all(sent, ALL, 0, 0, tiled=True)  10.5 us
    dot_general x2, matrix products, body(): jnp.dot(features, weights_bf, preferred_element_type=jnp.float32)  7.91 us
  transfers between devices with their start and end apart: 4, of which 3 were waited for; matrix products, arithmetic and copies ran while one was open for 3% of the time, Pallas kernels for 1%

profile of v1, /device:TPU:1, one launch (start us, length us, event | category | flops | bytes accessed | tf_op | source)
XLA Modules:
  0.0 352.8 jit_solution(14675378954687402832)
XLA Ops:
  7.2 0.9 compare_and_fusion
  8.9 1.8 fusion.10
  10.8 1.1 scatter_custom_fusion
  11.9 3.8 %fusion.6 = f32[1024,256]{1,0:T(8,128)S(1)} fusion(f32[1024,256]{1,0:T(8,128)S(1)} %scatter_custom_fusion, bf16[1024,2048]{1,0:T(8,128)(2,1)} %param.12, bf16[2048,256]{1,0:T(8,128)(2,1)S(1)} %copy-done.3), kind=kOutput, calls=%fused_computation.17 | convolution fusion | flops 1074266112 | bytes 7340032 | tf_op jit(solution)/shard_map/dot_general | solution.py:85
  15.8 47.4 %all_to_all.30 = f32[256,8,128]{2,1,0:T(8,128)S(1)} all-to-all(f32[256,8,128]{2,1,0:T(8,128)S(1)} %bitcast.58), channel_id=1, replica_groups=mesh['user'=16,'party'=16] {'user','party'}, dimensions={0} | all-to-all | bytes 2097152 | tf_op jit(solution)/shard_map/all_to_all | solution.py:22
  63.5 0.9 broadcast_in_dim.43
  64.4 5.2 %all-to-all-start.1 = ((bf16[256,8,128]{2,1,0:T(8,128)(2,1)}), bf16[256,8,128]{2,1,0:T(8,128)(2,1)S(1)}, u32[]{:S(2)}, u32[]{:S(2)}) async-start(bf16[256,8,128]{2,1,0:T(8,128)(2,1)} %broadcast_in_dim.43), calls=%async_computation.1 | async-start | bytes 1048576 | tf_op jit(solution)/shard_map/all_to_all | solution.py:28
  69.5 1.4 copy.13
  71.0 19.7 %all-to-all-done.1 = bf16[256,8,128]{2,1,0:T(8,128)(2,1)S(1)} async-done(((bf16[256,8,128]{2,1,0:T(8,128)(2,1)}), bf16[256,8,128]{2,1,0:T(8,128)(2,1)S(1)}, u32[]{:S(2)}, u32[]{:S(2)}) %all-to-all-start.1) | async-done | bytes 524320 | tf_op jit(solution)/shard_map/all_to_all | solution.py:28
  90.7 4.7 %multiply_reduce_fusion.1 = (f32[]{:T(128)}, f32[2048,256]{0,1:T(8,128)S(1)}) fusion(bf16[2048,256]{0,1:T(8,128)(2,1)} %copy.13, bf16[1024,256]{1,0:T(8,128)(2,1)S(1)} %bitcast.56, bf16[1024,2048]{1,0:T(8,128)(2,1)} %param.12), kind=kOutput, calls=%fused_computation.12 | convolution fusion | flops 1076887552 | bytes 7864324 | tf_op jit(solution)/shard_map/dot_general | solution.py:90
  96.2 18.1 %all_to_all.31 = f32[256,1,128]{2,1,0:T(1,128)S(1)} all-to-all(f32[256,1,128]{2,1,0:T(1,128)S(1)} %broadcast_in_dim.44), channel_id=1, replica_groups=mesh['user'=16,'party'=16] {'user','party'}, dimensions={0} | all-to-all | bytes 262144 | tf_op jit(solution)/shard_map/all_to_all | solution.py:34
  114.5 4.1 %fusion.7 = f32[1024,256]{1,0:T(8,128)S(1)} fusion(f32[1024,256]{1,0:T(8,128)} %copy-done.2, bf16[1024,2048]{1,0:T(8,128)(2,1)} %param.12, f32[2048,256]{0,1:T(8,128)S(1)} %get-tuple-element.9, bf16[2048,256]{0,1:T(8,128)(2,1)} %copy.13, f32[]{:T(128)} %bitcast.11), kind=kOutput, calls=%fused_computation.18 | convolution fusion | flops 1076363264 | bytes 9437188 | tf_op jit(solution)/shard_map/dot_general | solution.py:85
  118.5 38.5 %all_to_all.32 = f32[256,8,128]{2,1,0:T(8,128)} all-to-all(f32[256,8,128]{2,1,0:T(8,128)S(1)} %bitcast.55), channel_id=1, replica_groups=mesh['user'=16,'party'=16] {'user','party'}, dimensions={0} | all-to-all | bytes 2097152 | tf_op jit(solution)/shard_map/all_to_all | solution.py:22
  157.1 1.5 reduce_sum.62
  158.6 0.9 broadcast_in_dim.45
  159.4 5.3 %all-to-all-start.4 = ((bf16[256,8,128]{2,1,0:T(8,128)(2,1)}), bf16[256,8,128]{2,1,0:T(8,128)(2,1)S(1)}, u32[]{:S(2)}, u32[]{:S(2)}) async-start(bf16[256,8,128]{2,1,0:T(8,128)(2,1)} %broadcast_in_dim.45), calls=%async_computation.4 | async-start | bytes 1048576 | tf_op jit(solution)/shard_map/all_to_all | solution.py:28
  165.5 20.2 %all-to-all-done.4 = bf16[256,8,128]{2,1,0:T(8,128)(2,1)S(1)} async-done(((bf16[256,8,128]{2,1,0:T(8,128)(2,1)}), bf16[256,8,128]{2,1,0:T(8,128)(2,1)S(1)}, u32[]{:S(2)}, u32[]{:S(2)}) %all-to-all-start.4) | async-done | bytes 524320 | tf_op jit(solution)/shard_map/all_to_all | solution.py:28
  185.8 6.0 %multiply_reduce_fusion = (f32[]{:T(128)}, f32[2048,256]{0,1:T(8,128)}) fusion(f32[2048,256]{0,1:T(8,128)S(1)} %get-tuple-element.9, f32[]{:T(128)} %bitcast.11, bf16[2048,256]{0,1:T(8,128)(2,1)} %copy.13, bf16[1024,256]{1,0:T(8,128)(2,1)S(1)} %bitcast.57, bf16[1024,2048]{1,0:T(8,128)(2,1)} %param.12), kind=kOutput, calls=%fused_computation.11 | convolution fusion | flops 1077936128 | bytes 9961480 | tf_op jit(solution)/shard_map/dot_general | solution.py:90
  191.8 1.4 broadcast_in_dim.46
  193.2 5.5 %all-to-all-start.5 = ((f32[256,1,128]{2,1,0:T(1,128)}), f32[256,1,128]{2,1,0:T(1,128)S(1)}, u32[]{:S(2)}, u32[]{:S(2)}) async-start(f32[256,1,128]{2,1,0:T(1,128)} %broadcast_in_dim.46), calls=%async_computation.5 | async-start | bytes 262144 | tf_op jit(solution)/shard_map/all_to_all | solution.py:34
  198.7 137.7 %all-reduce.2.cloned.1.call-done = f32[64,256]{1,0:T(8,128)} async-done(((f32[64,256]{1,0:T(8,128)}), f32[64,256]{1,0:T(8,128)}) %all-reduce.2.cloned.1.call-update) | async-done | bytes 65552 | tf_op jit(solution)/shard_map/psum | solution.py:71
  336.3 1.5 convert_subtract_fusion.2
  337.9 4.2 %shard_map.86 = (f32[2048,256]{1,0:T(8,128)}, f32[2048,256]{1,0:T(8,128)}) custom-call(f32[1]{0:T(128)} %bitcast.9.scale_ref, bf16[2048,256]{1,0:T(8,128)(2,1)} %w_ref.1, f32[256,2048]{1,0:T(8,128)} %bitcast.53, f32[256,2048]{1,0:T(8,128)} %bitcast.54), custom_call_target="tpu_custom_call" | custom-call | tf_op jit(solution)/shard_map/pallas_call | solution.py:48
  342.2 3.8 %multiply_subtract_fusion = f32[2048,256]{1,0:T(8,128)} fusion(f32[2048,256]{1,0:T(8,128)} %get-tuple-element.4, f32[2048,256]{1,0:T(8,128)} %get-tuple-element.5, f32[]{:T(128)} %bitcast.23), kind=kLoop, calls=%fused_computation.10 | loop fusion | flops 1048576 | bytes 6291460 | tf_op jit(solution)/shard_map/sub | solution.py:104
  (19 shorter events, 2.7 us)
Async XLA Ops:
  7.2 1.1 copy-start
  7.2 4.7 %copy-start.3 = (bf16[2048,256]{1,0:T(8,128)(2,1)S(1)}, bf16[2048,256]{1,0:T(8,128)(2,1)}, u32[]{:S(2)}) copy-start(bf16[2048,256]{1,0:T(8,128)(2,1)} %w_ref.1) | copy-start | bytes 3145732
  10.8 5.0 %copy-start.4 = (f32[64,256]{1,0:T(8,128)}, f32[64,256]{1,0:T(8,128)S(1)}, u32[]{:S(2)}) copy-start(f32[64,256]{1,0:T(8,128)S(1)} %fusion.10) | copy-start | bytes 196612
  11.9 3.9 %copy-start.2 = (f32[1024,256]{1,0:T(8,128)}, f32[1024,256]{1,0:T(8,128)S(1)}, u32[]{:S(2)}) copy-start(f32[1024,256]{1,0:T(8,128)S(1)} %scatter_custom_fusion) | copy-start | bytes 3145732
  64.4 26.3 %all-to-all-start.1 = ((bf16[256,8,128]{2,1,0:T(8,128)(2,1)}), bf16[256,8,128]{2,1,0:T(8,128)(2,1)S(1)}, u32[]{:S(2)}, u32[]{:S(2)}) async-start(bf16[256,8,128]{2,1,0:T(8,128)(2,1)} %broadcast_in_dim.43), calls=%async_computation.1 | async-start | bytes 1048576 | tf_op jit(solution)/shard_map/all_to_all | solution.py:28
  95.4 90.3 %copy-start.1 = (f32[2048,256]{0,1:T(8,128)}, f32[2048,256]{0,1:T(8,128)S(1)}, u32[]{:S(2)}) copy-start(f32[2048,256]{0,1:T(8,128)S(1)} %get-tuple-element.9) | copy-start | bytes 6291460
  159.4 26.3 %all-to-all-start.4 = ((bf16[256,8,128]{2,1,0:T(8,128)(2,1)}), bf16[256,8,128]{2,1,0:T(8,128)(2,1)S(1)}, u32[]{:S(2)}, u32[]{:S(2)}) async-start(bf16[256,8,128]{2,1,0:T(8,128)(2,1)} %broadcast_in_dim.45), calls=%async_computation.4 | async-start | bytes 1048576 | tf_op jit(solution)/shard_map/all_to_all | solution.py:28
  164.8 171.6 %all-reduce.2.cloned.1.call-start = ((), (), s32[]{:S(2)}) async-start(), calls=%async_computation.6 | async-start | bytes 131072 | tf_op jit(solution)/shard_map/psum | solution.py:71
  193.2 148.9 %all-to-all-start.5 = ((f32[256,1,128]{2,1,0:T(1,128)}), f32[256,1,128]{2,1,0:T(1,128)S(1)}, u32[]{:S(2)}, u32[]{:S(2)}) async-start(f32[256,1,128]{2,1,0:T(1,128)} %broadcast_in_dim.46), calls=%async_computation.5 | async-start | bytes 262144 | tf_op jit(solution)/shard_map/all_to_all | solution.py:34
Sparse Core Ops, SparseCore 0:
  168.8 167.5 all-reduce.1

commit v2 on v1

--- a/solution.py
+++ b/solution.py
@@ -3,7 +3,7 @@
 from jax import lax
 from jax.experimental import pallas as pl
 from jax.experimental.pallas import tpu as pltpu
-from jax.sharding import PartitionSpec as P
+from jax.sharding import Mesh, PartitionSpec as P
 
 ITERS = 2
 
@@ -13,20 +13,44 @@
 ridge_decay = 0.05
 ridge_step = 0.05
 
-ALL = ("user", "party")
+USER = ("user_outer", "core")
+ALL = USER + ("party",)
+OTHERS = ("user_outer", "party")
 
 
-def reduce_scatter_tiles(x, n):
+def to_tiles(x, n):
     rows, cols = x.shape
-    tiles = x.reshape(rows // 8, 8, cols // 128, 128).transpose(0, 2, 1, 3).reshape(n, 8, 128)
-    return lax.all_to_all(tiles, ALL, 0, 0, tiled=True).sum(0)
+    return x.reshape(rows // 8, 8, cols // 128, 128).transpose(0, 2, 1, 3).reshape(n, 8, 128)
 
 
-def gather_tiles(block, n, shape):
+def from_tiles(tiles, shape):
     rows, cols = shape
+    return tiles.reshape(rows // 8, cols // 128, 8, 128).transpose(0, 2, 1, 3).reshape(rows, cols)
+
+
+def swap_cores(x):
+    return lax.ppermute(x, "core", [(0, 1), (1, 0)])
+
+
+def reduce_scatter_tiles(x):
+    core = lax.axis_index("core")
+    halves = x.reshape(2, x.shape[0] // 2, x.shape[1])
+    mine = lax.dynamic_index_in_dim(halves, core, 0, keepdims=False)
+    other = lax.dynamic_index_in_dim(halves, 1 - core, 0, keepdims=False)
+    half = mine + swap_cores(other)
+    n = lax.axis_size(OTHERS)
+    return lax.all_to_all(to_tiles(half, n), OTHERS, 0, 0, tiled=True).sum(0)
+
+
+def gather_tiles(block, shape):
+    core = lax.axis_index("core")
+    n = lax.axis_size(OTHERS)
     sent = jnp.broadcast_to(block[None], (n,) + block.shape)
-    got = lax.all_to_all(sent, ALL, 0, 0, tiled=True)
-    return got.reshape(rows // 8, cols // 128, 8, 128).transpose(0, 2, 1, 3).reshape(rows, cols)
+    half = from_tiles(lax.all_to_all(sent, OTHERS, 0, 0, tiled=True), (shape[0] // 2, shape[1]))
+    other = swap_cores(half)
+    low = jnp.where(core == 0, half, other)
+    high = jnp.where(core == 0, other, half)
+    return jnp.concatenate([low, high])
 
 
 def total_scalar(value, n):
@@ -57,7 +81,7 @@
 def body(ratings, rating_mask, user_factors, item_factors, item_index, features, ridge_weights):
     local_items = ratings.shape[0]
     party_pos = lax.axis_index("party")
-    user_pos = lax.axis_index("user")
+    user_pos = lax.axis_index(USER)
     devices_all = lax.axis_size(ALL)
     local_index = lax.dynamic_slice_in_dim(item_index, party_pos * local_items, local_items)
     tile_rows = jnp.take(item_factors, local_index, axis=0)
@@ -68,7 +92,7 @@
         jnp.bfloat16
     )
     partial_grad = jnp.dot(misfit, user_factors, preferred_element_type=jnp.float32)
-    grad_total = lax.psum(partial_grad, "user")
+    grad_total = lax.psum(partial_grad, USER)
     tile_wide = tile_rows.astype(jnp.float32)
     new_factors = tile_wide - learn_rate * (grad_total + factor_decay * tile_wide)
     own_tile = jnp.where(user_pos == 0, tile_wide - learn_rate * factor_decay * tile_wide, 0.0)
@@ -84,8 +108,8 @@
         partial_pred = (
             jnp.dot(features, weights_bf, preferred_element_type=jnp.float32) * feature_scale
         )
-        error_block = reduce_scatter_tiles(partial_pred + minus_targets, devices_all)
-        error_rows = gather_tiles(error_block.astype(jnp.bfloat16), devices_all, partial_pred.shape)
+        error_block = reduce_scatter_tiles(partial_pred + minus_targets)
+        error_rows = gather_tiles(error_block.astype(jnp.bfloat16), partial_pred.shape)
         grad = (
             lax.dot_general(
                 features, error_rows, (((0,), (0,)), ((), ())), preferred_element_type=jnp.float32
@@ -105,10 +129,13 @@
 
 
 def solution(mesh):
+    users = mesh.shape["user"]
+    grid = mesh.devices.reshape(users // 2, 2, mesh.shape["party"])
+    mesh = Mesh(grid, ("user_outer", "core", "party"))
     in_specs = (
-        P("party", "user"),
-        P("party", "user"),
-        P("user", None),
+        P("party", USER),
+        P("party", USER),
+        P(USER, None),
         P(),
         P(),
         P(None, ALL),

time: 354 us -> 333 us (0.941)
  waiting for transfers between devices: 178 us -> 149 us
  blocking collectives: 104 us -> 114 us
    all_to_all x2 -> x0, waiting for transfers between devices: 39.9 us -> none  [gather_tiles(): got = lax.all_to_all(sent, ALL, 0, 0, tiled=True)]
    all_to_all x2 -> x4, blocking collectives: 86 us -> 96.5 us  [the longest x2 57.6 us: reduce_scatter_tiles(): return lax.all_to_all(to_tiles(half, n), OTHERS, 0, 0, tiled=True).sum(0)]
    all_to_all x2 -> x0, starting transfers between devices: 10.5 us -> none  [gather_tiles(): got = lax.all_to_all(sent, ALL, 0, 0, tiled=True)]
    ppermute x0 -> x4, starting transfers between devices: none -> 10.4 us  [swap_cores(): return lax.ppermute(x, 'core', [(0, 1), (1, 0)])]
    psum x1, waiting for transfers between devices: 138 us -> 145 us  [body(): grad_total = lax.psum(partial_grad, USER)]
    ppermute x0 -> x4, waiting for transfers between devices: none -> 4.21 us  [swap_cores(): return lax.ppermute(x, 'core', [(0, 1), (1, 0)])]
  transfers between devices with their start and end apart: 4 -> 6, of which waited for: 3 -> 4; matrix products, arithmetic and copies ran while one was open for 3% -> 3% of each run, Pallas kernels for 1% -> 1%
where the time goes in v2:
time: 333 us; the launch traced here: 332 us
  waiting for transfers between devices  149 us (45%)
  blocking collectives  114 us (34%)
  matrix products  20.5 us (6%)
  starting transfers between devices  15.8 us (5%)
  between operations  14.4 us (4%)
  other arithmetic  9.03 us (3%)
  local copies, waits for them, and re-layouts  5.55 us (2%)
  Pallas kernels  4.16 us (1%)
    psum x1, waiting for transfers between devices, body(): grad_total = lax.psum(partial_grad, USER)  145 us
    all_to_all x2, blocking collectives, reduce_scatter_tiles(): return lax.all_to_all(to_tiles(half, n), OTHERS, 0, 0, tiled=True).sum(0)  57.6 us
    all_to_all x2, blocking collectives, gather_tiles(): lax.all_to_all(sent, OTHERS, 0, 0, tiled=True)  38.9 us
    all_to_all x1, blocking collectives, total_scalar(): return lax.all_to_all(sent, ALL, 0, 0, tiled=True).sum(0)[0, 0]  17.7 us
    dot_general x2, matrix products, body(): lax.dot_general(features, error_rows, (((0,), (0,)), ((), ())), preferred...  10.8 us
    ppermute x4, starting transfers between devices, swap_cores(): return lax.ppermute(x, 'core', [(0, 1), (1, 0)])  10.4 us
    dot_general x2, matrix products, body(): jnp.dot(features, weights_bf, preferred_element_type=jnp.float32)  7.86 us
  transfers between devices with their start and end apart: 6, of which 4 were waited for; matrix products, arithmetic and copies ran while one was open for 3% of the time, Pallas kernels for 1%

profile of v2, /device:TPU:1, one launch (start us, length us, event | category | flops | bytes accessed | tf_op | source)
XLA Modules:
  0.0 332.4 jit_solution(4581306034824683758)
XLA Ops:
  8.9 1.8 fusion.10
  10.8 1.1 scatter_custom_fusion
  12.0 3.8 %fusion.6 = f32[1024,256]{1,0:T(8,128)S(1)} fusion(f32[1024,256]{1,0:T(8,128)S(1)} %scatter_custom_fusion, bf16[1024,2048]{1,0:T(8,128)(2,1)} %param.12, bf16[2048,256]{1,0:T(8,128)(2,1)S(1)} %copy-done.3), kind=kOutput, calls=%fused_computation.17 | convolution fusion | flops 1074266112 | bytes 7340032 | tf_op jit(solution)/shard_map/dot_general | solution.py:109
  16.8 3.3 collective-permute-start
  20.1 1.5 collective-permute-done
  22.7 32.8 %all_to_all.30 = f32[128,8,128]{2,1,0:T(8,128)S(1)} all-to-all(f32[128,8,128]{2,1,0:T(8,128)S(1)} %bitcast.66), channel_id=1, replica_groups=mesh['user_outer'=8,'core'=2,'party'=16] {'user_outer','party'}, dimensions={0} | all-to-all | bytes 1048576 | tf_op jit(solution)/shard_map/all_to_all | solution.py:42
  55.7 19.3 %all_to_all.31 = bf16[128,8,128]{2,1,0:T(8,128)(2,1)S(1)} all-to-all(bf16[128,8,128]{2,1,0:T(8,128)(2,1)S(1)} %broadcast_in_dim.43), channel_id=1, replica_groups=mesh['user_outer'=8,'core'=2,'party'=16] {'user_outer','party'}, dimensions={0} | all-to-all | bytes 524288 | tf_op jit(solution)/shard_map/all_to_all | solution.py:49
  75.0 3.1 collective-permute-start.1
  78.1 1.4 copy.13
  79.6 4.7 %multiply_reduce_fusion.1 = (f32[]{:T(128)}, f32[2048,256]{0,1:T(8,128)S(1)}) fusion(bf16[2048,256]{0,1:T(8,128)(2,1)} %copy.13, bf16[1024,2048]{1,0:T(8,128)(2,1)} %param.12, bf16[512,256]{1,0:T(8,128)(2,1)S(1)} %get-tuple-element.11, bf16[512,256]{1,0:T(8,128)(2,1)S(1)} %get-tuple-element.10), kind=kOutput, calls=%fused_computation.12 | convolution fusion | flops 1077936128 | bytes 7864324 | tf_op jit(solution)/shard_map/dot_general | solution.py:114
  85.1 17.7 %all_to_all.32 = f32[256,1,128]{2,1,0:T(1,128)S(1)} all-to-all(f32[256,1,128]{2,1,0:T(1,128)S(1)} %broadcast_in_dim.44), channel_id=1, replica_groups=mesh['user_outer'=8,'core'=2,'party'=16] {'user_outer','core','party'}, dimensions={0} | all-to-all | bytes 262144 | tf_op jit(solution)/shard_map/all_to_all | solution.py:58
  103.0 4.1 %fusion.7 = f32[1024,256]{1,0:T(8,128)S(1)} fusion(f32[1024,256]{1,0:T(8,128)} %copy-done.2, bf16[1024,2048]{1,0:T(8,128)(2,1)} %param.12, f32[2048,256]{0,1:T(8,128)S(1)} %get-tuple-element.13, bf16[2048,256]{0,1:T(8,128)(2,1)} %copy.13, f32[]{:T(128)} %bitcast.16), kind=kOutput, calls=%fused_computation.18 | convolution fusion | flops 1076363264 | bytes 9437188 | tf_op jit(solution)/shard_map/dot_general | solution.py:109
  107.1 1.3 collective-permute-start.2
  108.4 1.5 collective-permute-done.2
  110.0 24.8 %all_to_all.33 = f32[128,8,128]{2,1,0:T(8,128)S(1)} all-to-all(f32[128,8,128]{2,1,0:T(8,128)S(1)} %bitcast.65), channel_id=1, replica_groups=mesh['user_outer'=8,'core'=2,'party'=16] {'user_outer','party'}, dimensions={0} | all-to-all | bytes 1048576 | tf_op jit(solution)/shard_map/all_to_all | solution.py:42
  135.0 19.6 %all_to_all.34 = bf16[128,8,128]{2,1,0:T(8,128)(2,1)S(1)} all-to-all(bf16[128,8,128]{2,1,0:T(8,128)(2,1)S(1)} %broadcast_in_dim.45), channel_id=1, replica_groups=mesh['user_outer'=8,'core'=2,'party'=16] {'user_outer','party'}, dimensions={0} | all-to-all | bytes 524288 | tf_op jit(solution)/shard_map/all_to_all | solution.py:49
  154.6 2.8 collective-permute-start.3
  158.6 6.0 %multiply_reduce_fusion = (f32[]{:T(128)}, f32[2048,256]{0,1:T(8,128)}) fusion(f32[2048,256]{0,1:T(8,128)S(1)} %get-tuple-element.13, f32[]{:T(128)} %bitcast.16, bf16[2048,256]{0,1:T(8,128)(2,1)} %copy.13, bf16[1024,2048]{1,0:T(8,128)(2,1)} %param.12, bf16[512,256]{1,0:T(8,128)(2,1)S(1)} %get-tuple-element.9, bf16[512,256]{1,0:T(8,128)(2,1)S(1)} %get-tuple-element.8), kind=kOutput, calls=%fused_computation.11 | convolution fusion | flops 1078984704 | bytes 9961480 | tf_op jit(solution)/shard_map/dot_general | solution.py:114
  164.7 1.4 broadcast_in_dim.46
  166.0 5.3 %all-to-all-start.5 = ((f32[256,1,128]{2,1,0:T(1,128)}), f32[256,1,128]{2,1,0:T(1,128)S(1)}, u32[]{:S(2)}, u32[]{:S(2)}) async-start(f32[256,1,128]{2,1,0:T(1,128)} %broadcast_in_dim.46), calls=%async_computation.5 | async-start | bytes 262144 | tf_op jit(solution)/shard_map/all_to_all | solution.py:58
  171.4 144.5 %all-reduce.2.cloned.1.call-done = f32[64,256]{1,0:T(8,128)} async-done(((f32[64,256]{1,0:T(8,128)}), f32[64,256]{1,0:T(8,128)}) %all-reduce.2.cloned.1.call-update) | async-done | bytes 65552 | tf_op jit(solution)/shard_map/psum | solution.py:95
  315.9 1.5 convert_subtract_fusion.2
  317.5 4.2 %shard_map.86 = (f32[2048,256]{1,0:T(8,128)}, f32[2048,256]{1,0:T(8,128)}) custom-call(f32[1]{0:T(128)} %bitcast.14.scale_ref, bf16[2048,256]{1,0:T(8,128)(2,1)} %w_ref.1, f32[256,2048]{1,0:T(8,128)} %bitcast.61, f32[256,2048]{1,0:T(8,128)} %bitcast.62), custom_call_target="tpu_custom_call" | custom-call | tf_op jit(solution)/shard_map/pallas_call | solution.py:72
  321.8 3.8 %multiply_subtract_fusion = f32[2048,256]{1,0:T(8,128)} fusion(f32[2048,256]{1,0:T(8,128)} %get-tuple-element.4, f32[2048,256]{1,0:T(8,128)} %get-tuple-element.5, f32[]{:T(128)} %bitcast.33), kind=kLoop, calls=%fused_computation.10 | loop fusion | flops 1048576 | bytes 6291460 | tf_op jit(solution)/shard_map/sub | solution.py:128
  (33 shorter events, 6.5 us)
Async XLA Ops:
  7.2 1.1 copy-start
  7.2 4.8 %copy-start.3 = (bf16[2048,256]{1,0:T(8,128)(2,1)S(1)}, bf16[2048,256]{1,0:T(8,128)(2,1)}, u32[]{:S(2)}) copy-start(bf16[2048,256]{1,0:T(8,128)(2,1)} %w_ref.1) | copy-start | bytes 3145732
  10.8 5.0 %copy-start.5 = (f32[64,256]{1,0:T(8,128)}, f32[64,256]{1,0:T(8,128)S(1)}, u32[]{:S(2)}) copy-start(f32[64,256]{1,0:T(8,128)S(1)} %fusion.10) | copy-start | bytes 196612
  11.9 3.9 %copy-start.2 = (f32[1024,256]{1,0:T(8,128)}, f32[1024,256]{1,0:T(8,128)S(1)}, u32[]{:S(2)}) copy-start(f32[1024,256]{1,0:T(8,128)S(1)} %scatter_custom_fusion) | copy-start | bytes 3145732
  11.9 304.0 %all-reduce.2.cloned.1.call-start = ((), (), s32[]{:S(2)}) async-start(), calls=%async_computation.6 | async-start | bytes 131072 | tf_op jit(solution)/shard_map/psum | solution.py:95
  15.8 1.0 copy-start.4
  16.8 4.8 %collective-permute-start = (f32[512,256]{1,0:T(8,128)S(1)}, f32[512,256]{1,0:T(8,128)S(1)}, u32[]{:S(2)}, u32[]{:S(2)}) collective-permute-start(f32[512,256]{1,0:T(8,128)S(1)} %dynamic-slice_bitcast_fusion.1), channel_id=1, source_target_pairs={{0,16},{16,0},{1,17},{17,1},{2,18},{18,2},{3,19},{19,3},{4,20},{20... | collective-permute-start | bytes 1572872 | tf_op jit(solution)/shard_map/ppermute | solution.py:32
  75.0 4.5 %collective-permute-start.1 = (bf16[512,256]{1,0:T(8,128)(2,1)S(1)}, bf16[512,256]{1,0:T(8,128)(2,1)S(1)}, u32[]{:S(2)}, u32[]{:S(2)}) collective-permute-start(bf16[512,256]{1,0:T(8,128)(2,1)S(1)} %bitcast.71), channel_id=1, source_target_pairs={{0,16},{16,0},{1,17},{17,1},{2,18},{18,2},{3,19},{19,3},{4,20},{20... | collective-permute-start | bytes 786440 | tf_op jit(solution)/shard_map/ppermute | solution.py:32
  84.3 74.3 %copy-start.1 = (f32[2048,256]{0,1:T(8,128)}, f32[2048,256]{0,1:T(8,128)S(1)}, u32[]{:S(2)}) copy-start(f32[2048,256]{0,1:T(8,128)S(1)} %get-tuple-element.13) | copy-start | bytes 6291460
  107.1 2.8 collective-permute-start.2
  154.6 3.9 %collective-permute-start.3 = (bf16[512,256]{1,0:T(8,128)(2,1)S(1)}, bf16[512,256]{1,0:T(8,128)(2,1)S(1)}, u32[]{:S(2)}, u32[]{:S(2)}) collective-permute-start(bf16[512,256]{1,0:T(8,128)(2,1)S(1)} %bitcast.69), channel_id=1, source_target_pairs={{0,16},{16,0},{1,17},{17,1},{2,18},{18,2},{3,19},{19,3},{4,20},{20... | collective-permute-start | bytes 786440 | tf_op jit(solution)/shard_map/ppermute | solution.py:32
  166.0 155.6 %all-to-all-start.5 = ((f32[256,1,128]{2,1,0:T(1,128)}), f32[256,1,128]{2,1,0:T(1,128)S(1)}, u32[]{:S(2)}, u32[]{:S(2)}) async-start(f32[256,1,128]{2,1,0:T(1,128)} %broadcast_in_dim.46), calls=%async_computation.5 | async-start | bytes 262144 | tf_op jit(solution)/shard_map/all_to_all | solution.py:58
Sparse Core Ops, SparseCore 0:
  157.5 158.3 all-reduce.1

commit v3 on v2

--- a/solution.py
+++ b/solution.py
@@ -14,8 +14,9 @@
 ridge_step = 0.05
 
 USER = ("user_outer", "core")
-ALL = USER + ("party",)
-OTHERS = ("user_outer", "party")
+PARTY = ("x_outer", "x_pair", "party_inner")
+ALL = USER + PARTY
+OTHERS = ("user_outer", "x_outer", "party_inner")
 
 
 def to_tiles(x, n):
@@ -28,29 +29,37 @@
     return tiles.reshape(rows // 8, cols // 128, 8, 128).transpose(0, 2, 1, 3).reshape(rows, cols)
 
 
-def swap_cores(x):
-    return lax.ppermute(x, "core", [(0, 1), (1, 0)])
+def swap(x, axis):
+    return lax.ppermute(x, axis, [(0, 1), (1, 0)])
+
+
+def halve(x, axis):
+    side = lax.axis_index(axis)
+    halves = x.reshape(2, x.shape[0] // 2, x.shape[1])
+    mine = lax.dynamic_index_in_dim(halves, side, 0, keepdims=False)
+    other = lax.dynamic_index_in_dim(halves, 1 - side, 0, keepdims=False)
+    return mine + swap(other, axis)
+
+
+def double(x, axis):
+    side = lax.axis_index(axis)
+    other = swap(x, axis)
+    low = jnp.where(side == 0, x, other)
+    high = jnp.where(side == 0, other, x)
+    return jnp.concatenate([low, high])
 
 
 def reduce_scatter_tiles(x):
-    core = lax.axis_index("core")
-    halves = x.reshape(2, x.shape[0] // 2, x.shape[1])
-    mine = lax.dynamic_index_in_dim(halves, core, 0, keepdims=False)
-    other = lax.dynamic_index_in_dim(halves, 1 - core, 0, keepdims=False)
-    half = mine + swap_cores(other)
+    part = halve(halve(x, "core"), "x_pair")
     n = lax.axis_size(OTHERS)
-    return lax.all_to_all(to_tiles(half, n), OTHERS, 0, 0, tiled=True).sum(0)
+    return lax.all_to_all(to_tiles(part, n), OTHERS, 0, 0, tiled=True).sum(0)
 
 
 def gather_tiles(block, shape):
-    core = lax.axis_index("core")
     n = lax.axis_size(OTHERS)
     sent = jnp.broadcast_to(block[None], (n,) + block.shape)
-    half = from_tiles(lax.all_to_all(sent, OTHERS, 0, 0, tiled=True), (shape[0] // 2, shape[1]))
-    other = swap_cores(half)
-    low = jnp.where(core == 0, half, other)
-    high = jnp.where(core == 0, other, half)
-    return jnp.concatenate([low, high])
+    part = from_tiles(lax.all_to_all(sent, OTHERS, 0, 0, tiled=True), (shape[0] // 4, shape[1]))
+    return double(double(part, "x_pair"), "core")
 
 
 def total_scalar(value, n):
@@ -80,7 +89,7 @@
 
 def body(ratings, rating_mask, user_factors, item_factors, item_index, features, ridge_weights):
     local_items = ratings.shape[0]
-    party_pos = lax.axis_index("party")
+    party_pos = lax.axis_index(PARTY)
     user_pos = lax.axis_index(USER)
     devices_all = lax.axis_size(ALL)
     local_index = lax.dynamic_slice_in_dim(item_index, party_pos * local_items, local_items)
@@ -130,16 +139,17 @@
 
 def solution(mesh):
     users = mesh.shape["user"]
-    grid = mesh.devices.reshape(users // 2, 2, mesh.shape["party"])
-    mesh = Mesh(grid, ("user_outer", "core", "party"))
+    parties = mesh.shape["party"]
+    grid = mesh.devices.reshape(users // 2, 2, 2, 2, parties // 4)
+    mesh = Mesh(grid, USER + PARTY)
     in_specs = (
-        P("party", USER),
-        P("party", USER),
+        P(PARTY, USER),
+        P(PARTY, USER),
         P(USER, None),
         P(),
         P(),
         P(None, ALL),
         P(ALL, None),
     )
-    out_specs = (P("party", None), P(ALL, None))
+    out_specs = (P(PARTY, None), P(ALL, None))
     return jax.shard_map(body, mesh=mesh, in_specs=in_specs, out_specs=out_specs, check_vma=False)

time: 333 us -> 339 us (1.018)
  waiting for transfers between devices: 149 us -> 170 us
  blocking collectives: 114 us -> 94.4 us
  starting transfers between devices: 15.8 us -> 19.8 us
    ppermute x4 -> x8, waiting for transfers between devices: 4.21 us -> 25.8 us  [swap(): return lax.ppermute(x, axis, [(0, 1), (1, 0)])]
    all_to_all x2, blocking collectives: 57.6 us -> 42.6 us  [reduce_scatter_tiles(): return lax.all_to_all(to_tiles(part, n), OTHERS, 0, 0, tiled=True).sum(0)]
    all_to_all x2, blocking collectives: 38.9 us -> 34.1 us  [gather_tiles(): lax.all_to_all(sent, OTHERS, 0, 0, tiled=True)]
    ppermute x4 -> x8, starting transfers between devices: 10.4 us -> 14.3 us  [swap(): return lax.ppermute(x, axis, [(0, 1), (1, 0)])]
  transfers between devices with their start and end apart: 6 -> 10, of which waited for: 4 -> 8; matrix products, arithmetic and copies ran while one was open for 3% -> 3% of each run, Pallas kernels for 1% -> 1%
where the time goes in v3:
time: 339 us; the launch traced here: 338 us
  waiting for transfers between devices  170 us (50%)
  blocking collectives  94.4 us (28%)
  matrix products  20.4 us (6%)
  starting transfers between devices  19.8 us (6%)
  between operations  14.4 us (4%)
  other arithmetic  9.14 us (3%)
  local copies, waits for them, and re-layouts  5.52 us (2%)
  Pallas kernels  4.18 us (1%)
    psum x1, waiting for transfers between devices, body(): grad_total = lax.psum(partial_grad, USER)  144 us
    all_to_all x2, blocking collectives, reduce_scatter_tiles(): return lax.all_to_all(to_tiles(part, n), OTHERS, 0, 0, tiled=True).sum(0)  42.6 us
    all_to_all x2, blocking collectives, gather_tiles(): lax.all_to_all(sent, OTHERS, 0, 0, tiled=True)  34.1 us
    ppermute x8, waiting for transfers between devices, swap(): return lax.ppermute(x, axis, [(0, 1), (1, 0)])  25.8 us
    all_to_all x1, blocking collectives, total_scalar(): return lax.all_to_all(sent, ALL, 0, 0, tiled=True).sum(0)[0, 0]  17.7 us
    ppermute x8, starting transfers between devices, swap(): return lax.ppermute(x, axis, [(0, 1), (1, 0)])  14.3 us
    dot_general x2, matrix products, body(): lax.dot_general(features, error_rows, (((0,), (0,)), ((), ())), preferred...  10.8 us
    dot_general x2, matrix products, body(): jnp.dot(features, weights_bf, preferred_element_type=jnp.float32)  7.86 us
  transfers between devices with their start and end apart: 10, of which 8 were waited for; matrix products, arithmetic and copies ran while one was open for 3% of the time, Pallas kernels for 1%

profile of v3, /device:TPU:1, one launch (start us, length us, event | category | flops | bytes accessed | tf_op | source)
XLA Modules:
  0.0 338.0 jit_solution(18424916994932058366)
XLA Ops:
  8.9 1.8 fusion.10
  12.0 3.8 %fusion.6 = f32[1024,256]{1,0:T(8,128)S(1)} fusion(f32[1024,256]{1,0:T(8,128)S(1)} %scatter_custom_fusion, bf16[1024,2048]{1,0:T(8,128)(2,1)} %param.12, bf16[2048,256]{1,0:T(8,128)(2,1)S(1)} %copy-done.3), kind=kOutput, calls=%fused_computation.17 | convolution fusion | flops 1074266112 | bytes 7340032 | tf_op jit(solution)/shard_map/dot_general | solution.py:118
  16.8 3.3 collective-permute-start
  20.1 1.5 collective-permute-done
  22.9 7.5 %collective-permute-done.1 = f32[256,256]{1,0:T(8,128)S(1)} collective-permute-done((f32[256,256]{1,0:T(8,128)S(1)}, f32[256,256]{1,0:T(8,128)S(1)}, u32[]{:S(2)}, u32[]{:S(2)}) %collective-permute-start.1) | collective-permute-done | bytes 262176 | tf_op jit(solution)/shard_map/ppermute | solution.py:33
  30.4 25.3 %all_to_all.30 = f32[64,8,128]{2,1,0:T(8,128)S(1)} all-to-all(f32[64,8,128]{2,1,0:T(8,128)S(1)} %bitcast.82), channel_id=1, replica_groups=mesh['user_outer'=8,'core'=2,'x_outer'=2,'x_pair'=2,'party_inner'=4] {'u..., dimensions={0} | all-to-all | bytes 524288 | tf_op jit(solution)/shard_map/all_to_all | solution.py:55
  55.8 17.1 %all_to_all.31 = bf16[64,8,128]{2,1,0:T(8,128)(2,1)S(1)} all-to-all(bf16[64,8,128]{2,1,0:T(8,128)(2,1)S(1)} %broadcast_in_dim.43), channel_id=1, replica_groups=mesh['user_outer'=8,'core'=2,'x_outer'=2,'x_pair'=2,'party_inner'=4] {'u..., dimensions={0} | all-to-all | bytes 262144 | tf_op jit(solution)/shard_map/all_to_all | solution.py:61
  73.1 3.5 %collective-permute-done.2 = bf16[256,256]{1,0:T(8,128)(2,1)S(1)} collective-permute-done((bf16[256,256]{1,0:T(8,128)(2,1)S(1)}, bf16[256,256]{1,0:T(8,128)(2,1)S(1)}, u32[]{:S(2)}, u32[]{:S(2)}) %collective-permute-start.2) | collective-permute-done | bytes 131104 | tf_op jit(solution)/shard_map/ppermute | solution.py:33
  76.7 4.3 %collective-permute-start.3 = (bf16[512,256]{1,0:T(8,128)(2,1)S(1)}, bf16[512,256]{1,0:T(8,128)(2,1)S(1)}, u32[]{:S(2)}, u32[]{:S(2)}) collective-permute-start(bf16[512,256]{1,0:T(8,128)(2,1)S(1)} %pad_maximum_fusion), channel_id=1, source_target_pairs={{0,16},{16,0},{1,17},{17,1},{2,18},{18,2},{3,19},{19,3},{4,20},{20... | collective-permute-start | bytes 786440 | tf_op jit(solution)/shard_map/ppermute | solution.py:33
  82.6 4.7 %multiply_reduce_fusion.1 = (f32[]{:T(128)}, f32[2048,256]{0,1:T(8,128)S(1)}) fusion(bf16[2048,256]{0,1:T(8,128)(2,1)} %copy.13, bf16[1024,2048]{1,0:T(8,128)(2,1)} %param.12, bf16[512,256]{1,0:T(8,128)(2,1)S(1)} %get-tuple-element.11, bf16[512,256]{1,0:T(8,128)(2,1)S(1)} %get-tuple-element.10), kind=kOutput, calls=%fused_computation.12 | convolution fusion | flops 1077936128 | bytes 7864324 | tf_op jit(solution)/shard_map/dot_general | solution.py:123
  88.1 17.7 %all_to_all.32 = f32[256,1,128]{2,1,0:T(1,128)S(1)} all-to-all(f32[256,1,128]{2,1,0:T(1,128)S(1)} %broadcast_in_dim.44), channel_id=1, replica_groups=mesh['user_outer'=8,'core'=2,'x_outer'=2,'x_pair'=2,'party_inner'=4] {'u..., dimensions={0} | all-to-all | bytes 262144 | tf_op jit(solution)/shard_map/all_to_all | solution.py:67
  105.9 4.1 %fusion.7 = f32[1024,256]{1,0:T(8,128)S(1)} fusion(f32[1024,256]{1,0:T(8,128)} %copy-done.2, bf16[1024,2048]{1,0:T(8,128)(2,1)} %param.12, f32[2048,256]{0,1:T(8,128)S(1)} %get-tuple-element.17, bf16[2048,256]{0,1:T(8,128)(2,1)} %copy.13, f32[]{:T(128)} %bitcast.19), kind=kOutput, calls=%fused_computation.18 | convolution fusion | flops 1076363264 | bytes 9437188 | tf_op jit(solution)/shard_map/dot_general | solution.py:118
  111.2 1.5 collective-permute-done.4
  113.4 7.2 %collective-permute-done.5 = f32[256,256]{1,0:T(8,128)S(1)} collective-permute-done((f32[256,256]{1,0:T(8,128)S(1)}, f32[256,256]{1,0:T(8,128)S(1)}, u32[]{:S(2)}, u32[]{:S(2)}) %collective-permute-start.5) | collective-permute-done | bytes 262176 | tf_op jit(solution)/shard_map/ppermute | solution.py:33
  120.6 17.3 %all_to_all.33 = f32[64,8,128]{2,1,0:T(8,128)S(1)} all-to-all(f32[64,8,128]{2,1,0:T(8,128)S(1)} %bitcast.81), channel_id=1, replica_groups=mesh['user_outer'=8,'core'=2,'x_outer'=2,'x_pair'=2,'party_inner'=4] {'u..., dimensions={0} | all-to-all | bytes 524288 | tf_op jit(solution)/shard_map/all_to_all | solution.py:55
  138.0 17.0 %all_to_all.34 = bf16[64,8,128]{2,1,0:T(8,128)(2,1)S(1)} all-to-all(bf16[64,8,128]{2,1,0:T(8,128)(2,1)S(1)} %broadcast_in_dim.45), channel_id=1, replica_groups=mesh['user_outer'=8,'core'=2,'x_outer'=2,'x_pair'=2,'party_inner'=4] {'u..., dimensions={0} | all-to-all | bytes 262144 | tf_op jit(solution)/shard_map/all_to_all | solution.py:61
  155.5 3.4 collective-permute-done.6
  158.9 4.2 %collective-permute-start.7 = (bf16[512,256]{1,0:T(8,128)(2,1)S(1)}, bf16[512,256]{1,0:T(8,128)(2,1)S(1)}, u32[]{:S(2)}, u32[]{:S(2)}) collective-permute-start(bf16[512,256]{1,0:T(8,128)(2,1)S(1)} %pad_maximum_fusion.1), channel_id=1, source_target_pairs={{0,16},{16,0},{1,17},{17,1},{2,18},{18,2},{3,19},{19,3},{4,20},{20... | collective-permute-start | bytes 786440 | tf_op jit(solution)/shard_map/ppermute | solution.py:33
  164.4 6.0 %multiply_reduce_fusion = (f32[]{:T(128)}, f32[2048,256]{0,1:T(8,128)}) fusion(f32[2048,256]{0,1:T(8,128)S(1)} %get-tuple-element.17, f32[]{:T(128)} %bitcast.19, bf16[2048,256]{0,1:T(8,128)(2,1)} %copy.13, bf16[1024,2048]{1,0:T(8,128)(2,1)} %param.12, bf16[512,256]{1,0:T(8,128)(2,1)S(1)} %get-tuple-element.9, bf16[512,256]{1,0:T(8,128)(2,1)S(1)} %get-tuple-element.8), kind=kOutput, calls=%fused_computation.11 | convolution fusion | flops 1078984704 | bytes 9961480 | tf_op jit(solution)/shard_map/dot_general | solution.py:123
  171.7 5.4 %all-to-all-start.5 = ((f32[256,1,128]{2,1,0:T(1,128)}), f32[256,1,128]{2,1,0:T(1,128)S(1)}, u32[]{:S(2)}, u32[]{:S(2)}) async-start(f32[256,1,128]{2,1,0:T(1,128)} %broadcast_in_dim.46), calls=%async_computation.5 | async-start | bytes 262144 | tf_op jit(solution)/shard_map/all_to_all | solution.py:67
  177.1 144.3 %all-reduce.2.cloned.1.call-done = f32[64,256]{1,0:T(8,128)} async-done(((f32[64,256]{1,0:T(8,128)}), f32[64,256]{1,0:T(8,128)}) %all-reduce.2.cloned.1.call-update) | async-done | bytes 65552 | tf_op jit(solution)/shard_map/psum | solution.py:104
  321.5 1.5 convert_subtract_fusion.2
  323.0 4.2 %shard_map.86 = (f32[2048,256]{1,0:T(8,128)}, f32[2048,256]{1,0:T(8,128)}) custom-call(f32[1]{0:T(128)} %bitcast.17.scale_ref, bf16[2048,256]{1,0:T(8,128)(2,1)} %w_ref.1, f32[256,2048]{1,0:T(8,128)} %bitcast.71, f32[256,2048]{1,0:T(8,128)} %bitcast.72), custom_call_target="tpu_custom_call" | custom-call | tf_op jit(solution)/shard_map/pallas_call | solution.py:81
  327.3 3.8 %multiply_subtract_fusion = f32[2048,256]{1,0:T(8,128)} fusion(f32[2048,256]{1,0:T(8,128)} %get-tuple-element.4, f32[2048,256]{1,0:T(8,128)} %get-tuple-element.5, f32[]{:T(128)} %bitcast.39), kind=kLoop, calls=%fused_computation.10 | loop fusion | flops 1048576 | bytes 6291460 | tf_op jit(solution)/shard_map/sub | solution.py:137
  (49 shorter events, 13.0 us)
Async XLA Ops:
  7.2 1.1 copy-start
  7.2 4.8 %copy-start.3 = (bf16[2048,256]{1,0:T(8,128)(2,1)S(1)}, bf16[2048,256]{1,0:T(8,128)(2,1)}, u32[]{:S(2)}) copy-start(bf16[2048,256]{1,0:T(8,128)(2,1)} %w_ref.1) | copy-start | bytes 3145732
  10.8 5.0 %copy-start.5 = (f32[64,256]{1,0:T(8,128)}, f32[64,256]{1,0:T(8,128)S(1)}, u32[]{:S(2)}) copy-start(f32[64,256]{1,0:T(8,128)S(1)} %fusion.10) | copy-start | bytes 196612
  11.9 3.9 %copy-start.2 = (f32[1024,256]{1,0:T(8,128)}, f32[1024,256]{1,0:T(8,128)S(1)}, u32[]{:S(2)}) copy-start(f32[1024,256]{1,0:T(8,128)S(1)} %scatter_custom_fusion) | copy-start | bytes 3145732
  11.9 309.5 %all-reduce.2.cloned.1.call-start = ((), (), s32[]{:S(2)}) async-start(), calls=%async_computation.6 | async-start | bytes 131072 | tf_op jit(solution)/shard_map/psum | solution.py:104
  15.8 1.0 copy-start.4
  16.8 4.8 %collective-permute-start = (f32[512,256]{1,0:T(8,128)S(1)}, f32[512,256]{1,0:T(8,128)S(1)}, u32[]{:S(2)}, u32[]{:S(2)}) collective-permute-start(f32[512,256]{1,0:T(8,128)S(1)} %dynamic-slice_bitcast_fusion.1), channel_id=1, source_target_pairs={{0,16},{16,0},{1,17},{17,1},{2,18},{18,2},{3,19},{19,3},{4,20},{20... | collective-permute-start | bytes 1572872 | tf_op jit(solution)/shard_map/ppermute | solution.py:33
  22.8 7.6 %collective-permute-start.1 = (f32[256,256]{1,0:T(8,128)S(1)}, f32[256,256]{1,0:T(8,128)S(1)}, u32[]{:S(2)}, u32[]{:S(2)}) collective-permute-start(f32[256,256]{1,0:T(8,128)S(1)} %dynamic-slice_bitcast_fusion.3), channel_id=1, source_target_pairs={{0,4},{4,0},{1,5},{5,1},{2,6},{6,2},{3,7},{7,3},{8,12},{12,8},{9,1... | collective-permute-start | bytes 786440 | tf_op jit(solution)/shard_map/ppermute | solution.py:33
  72.8 3.8 %collective-permute-start.2 = (bf16[256,256]{1,0:T(8,128)(2,1)S(1)}, bf16[256,256]{1,0:T(8,128)(2,1)S(1)}, u32[]{:S(2)}, u32[]{:S(2)}) collective-permute-start(bf16[256,256]{1,0:T(8,128)(2,1)S(1)} %bitcast.83), channel_id=1, source_target_pairs={{0,4},{4,0},{1,5},{5,1},{2,6},{6,2},{3,7},{7,3},{8,12},{12,8},{9,1... | collective-permute-start | bytes 393224 | tf_op jit(solution)/shard_map/ppermute | solution.py:33
  76.7 5.8 %collective-permute-start.3 = (bf16[512,256]{1,0:T(8,128)(2,1)S(1)}, bf16[512,256]{1,0:T(8,128)(2,1)S(1)}, u32[]{:S(2)}, u32[]{:S(2)}) collective-permute-start(bf16[512,256]{1,0:T(8,128)(2,1)S(1)} %pad_maximum_fusion), channel_id=1, source_target_pairs={{0,16},{16,0},{1,17},{17,1},{2,18},{18,2},{3,19},{19,3},{4,20},{20... | collective-permute-start | bytes 786440 | tf_op jit(solution)/shard_map/ppermute | solution.py:33
  87.3 77.0 %copy-start.1 = (f32[2048,256]{0,1:T(8,128)}, f32[2048,256]{0,1:T(8,128)S(1)}, u32[]{:S(2)}) copy-start(f32[2048,256]{0,1:T(8,128)S(1)} %get-tuple-element.17) | copy-start | bytes 6291460
  110.1 2.6 collective-permute-start.4
  112.8 7.8 %collective-permute-start.5 = (f32[256,256]{1,0:T(8,128)S(1)}, f32[256,256]{1,0:T(8,128)S(1)}, u32[]{:S(2)}, u32[]{:S(2)}) collective-permute-start(f32[256,256]{1,0:T(8,128)S(1)} %dynamic-slice_bitcast_fusion.2), channel_id=1, source_target_pairs={{0,4},{4,0},{1,5},{5,1},{2,6},{6,2},{3,7},{7,3},{8,12},{12,8},{9,1... | collective-permute-start | bytes 786440 | tf_op jit(solution)/shard_map/ppermute | solution.py:33
  155.0 3.8 %collective-permute-start.6 = (bf16[256,256]{1,0:T(8,128)(2,1)S(1)}, bf16[256,256]{1,0:T(8,128)(2,1)S(1)}, u32[]{:S(2)}, u32[]{:S(2)}) collective-permute-start(bf16[256,256]{1,0:T(8,128)(2,1)S(1)} %bitcast.85), channel_id=1, source_target_pairs={{0,4},{4,0},{1,5},{5,1},{2,6},{6,2},{3,7},{7,3},{8,12},{12,8},{9,1... | collective-permute-start | bytes 393224 | tf_op jit(solution)/shard_map/ppermute | solution.py:33
  158.9 5.3 %collective-permute-start.7 = (bf16[512,256]{1,0:T(8,128)(2,1)S(1)}, bf16[512,256]{1,0:T(8,128)(2,1)S(1)}, u32[]{:S(2)}, u32[]{:S(2)}) collective-permute-start(bf16[512,256]{1,0:T(8,128)(2,1)S(1)} %pad_maximum_fusion.1), channel_id=1, source_target_pairs={{0,16},{16,0},{1,17},{17,1},{2,18},{18,2},{3,19},{19,3},{4,20},{20... | collective-permute-start | bytes 786440 | tf_op jit(solution)/shard_map/ppermute | solution.py:33
  171.7 155.5 %all-to-all-start.5 = ((f32[256,1,128]{2,1,0:T(1,128)}), f32[256,1,128]{2,1,0:T(1,128)S(1)}, u32[]{:S(2)}, u32[]{:S(2)}) async-start(f32[256,1,128]{2,1,0:T(1,128)} %broadcast_in_dim.46), calls=%async_computation.5 | async-start | bytes 262144 | tf_op jit(solution)/shard_map/all_to_all | solution.py:67
Sparse Core Ops, SparseCore 0:
  163.2 158.1 all-reduce.1

commit v4 on v2

--- a/solution.py
+++ b/solution.py
@@ -101,10 +101,11 @@
     minus_targets = jnp.zeros((items, share.shape[1]), jnp.float32).at[local_index].set(share)
     total_features = features.shape[1] * devices_all
     feature_scale = 1.0 / float(total_features) ** 0.5
-    weights = ridge_weights.astype(jnp.float32)
+    weights_t = lax.optimization_barrier(ridge_weights.T)
+    weights = weights_t.T.astype(jnp.float32)
     grads, scales = [], []
     for iteration in range(ITERS):
-        weights_bf = weights.astype(jnp.bfloat16)
+        weights_bf = ridge_weights if iteration == 0 else weights.astype(jnp.bfloat16)
         partial_pred = (
             jnp.dot(features, weights_bf, preferred_element_type=jnp.float32) * feature_scale
         )

time: 333 us -> 334 us (level)
  transfers between devices with their start and end apart: 6 -> 6, of which waited for: 4 -> 5; matrix products, arithmetic and copies ran while one was open for 3% -> 3% of each run, Pallas kernels for 1% -> 1%
where the time goes in v4:
time: 334 us; the launch traced here: 333 us
  waiting for transfers between devices  147 us (44%)
  blocking collectives  115 us (34%)
  matrix products  22 us (7%)
  starting transfers between devices  15.8 us (5%)
  between operations  14.4 us (4%)
  other arithmetic  10.2 us (3%)
  local copies, waits for them, and re-layouts  4.74 us (1%)
  Pallas kernels  4.19 us (1%)
    psum x1, waiting for transfers between devices, body(): grad_total = lax.psum(partial_grad, USER)  143 us
    all_to_all x2, blocking collectives, reduce_scatter_tiles(): return lax.all_to_all(to_tiles(half, n), OTHERS, 0, 0, tiled=True).sum(0)  57.6 us
    all_to_all x2, blocking collectives, gather_tiles(): lax.all_to_all(sent, OTHERS, 0, 0, tiled=True)  38.9 us
    all_to_all x1, blocking collectives, total_scalar(): return lax.all_to_all(sent, ALL, 0, 0, tiled=True).sum(0)[0, 0]  18 us
    dot_general x2, matrix products, body(): lax.dot_general(features, error_rows, (((0,), (0,)), ((), ())), preferred...  12.3 us
    ppermute x4, starting transfers between devices, swap_cores(): return lax.ppermute(x, 'core', [(0, 1), (1, 0)])  10.5 us
    dot_general x2, matrix products, body(): jnp.dot(features, weights_bf, preferred_element_type=jnp.float32)  7.93 us
  transfers between devices with their start and end apart: 6, of which 5 were waited for; matrix products, arithmetic and copies ran while one was open for 3% of the time, Pallas kernels for 1%

profile of v4, /device:TPU:1, one launch (start us, length us, event | category | flops | bytes accessed | tf_op | source)
XLA Modules:
  0.0 333.4 jit_solution(11718465806095440024)
XLA Ops:
  8.9 1.8 fusion.13
  10.8 1.1 scatter_custom_fusion
  12.0 3.8 %fusion.9 = f32[1024,256]{1,0:T(8,128)S(1)} fusion(f32[1024,256]{1,0:T(8,128)S(1)} %scatter_custom_fusion, bf16[1024,2048]{1,0:T(8,128)(2,1)} %param.12, bf16[2048,256]{1,0:T(8,128)(2,1)S(1)} %copy-done.2), kind=kOutput, calls=%fused_computation.21 | convolution fusion | flops 1074266112 | bytes 7340032 | tf_op jit(solution)/shard_map/dot_general | solution.py:110
  16.8 3.3 collective-permute-start
  20.1 1.5 collective-permute-done
  22.7 32.8 %all_to_all.30 = f32[128,8,128]{2,1,0:T(8,128)S(1)} all-to-all(f32[128,8,128]{2,1,0:T(8,128)S(1)} %bitcast.91), channel_id=1, replica_groups=mesh['user_outer'=8,'core'=2,'party'=16] {'user_outer','party'}, dimensions={0} | all-to-all | bytes 1048576 | tf_op jit(solution)/shard_map/all_to_all | solution.py:42
  55.7 19.3 %all_to_all.31 = bf16[128,8,128]{2,1,0:T(8,128)(2,1)S(1)} all-to-all(bf16[128,8,128]{2,1,0:T(8,128)(2,1)S(1)} %broadcast_in_dim.43), channel_id=1, replica_groups=mesh['user_outer'=8,'core'=2,'party'=16] {'user_outer','party'}, dimensions={0} | all-to-all | bytes 524288 | tf_op jit(solution)/shard_map/all_to_all | solution.py:49
  75.0 3.1 collective-permute-start.1
  79.3 5.6 %multiply_reduce_fusion = (f32[]{:T(128)}, f32[256,2048]{1,0:T(8,128)}) fusion(bf16[256,2048]{1,0:T(8,128)(2,1)S(1)} %bitcast.86, bf16[1024,2048]{1,0:T(8,128)(2,1)} %param.12, bf16[512,256]{1,0:T(8,128)(2,1)S(1)} %get-tuple-element.13, bf16[512,256]{1,0:T(8,128)(2,1)S(1)} %get-tuple-element.12), kind=kOutput, calls=%fused_computation.17 | convolution fusion | flops 1077936128 | bytes 7864324 | tf_op jit(solution)/shard_map/dot_general | solution.py:115
  85.8 18.0 %all_to_all.32 = f32[256,1,128]{2,1,0:T(1,128)S(1)} all-to-all(f32[256,1,128]{2,1,0:T(1,128)S(1)} %broadcast_in_dim.44), channel_id=1, replica_groups=mesh['user_outer'=8,'core'=2,'party'=16] {'user_outer','core','party'}, dimensions={0} | all-to-all | bytes 262144 | tf_op jit(solution)/shard_map/all_to_all | solution.py:58
  103.9 4.2 %fusion.10 = f32[1024,256]{1,0:T(8,128)S(1)} fusion(f32[1024,256]{1,0:T(8,128)S(1)} %copy-done.4, bf16[1024,2048]{1,0:T(8,128)(2,1)} %param.12, f32[256,2048]{1,0:T(8,128)} %get-tuple-element.15, bf16[256,2048]{1,0:T(8,128)(2,1)S(1)} %bitcast.87, f32[]{:T(128)} %bitcast.17), kind=kOutput, calls=%fused_computation.22 | convolution fusion | flops 1077411840 | bytes 9437188 | tf_op jit(solution)/shard_map/dot_general | solution.py:110
  108.1 1.3 collective-permute-start.2
  109.4 1.5 collective-permute-done.2
  111.0 24.8 %all_to_all.33 = f32[128,8,128]{2,1,0:T(8,128)S(1)} all-to-all(f32[128,8,128]{2,1,0:T(8,128)S(1)} %bitcast.90), channel_id=1, replica_groups=mesh['user_outer'=8,'core'=2,'party'=16] {'user_outer','party'}, dimensions={0} | all-to-all | bytes 1048576 | tf_op jit(solution)/shard_map/all_to_all | solution.py:42
  136.0 19.6 %all_to_all.34 = bf16[128,8,128]{2,1,0:T(8,128)(2,1)S(1)} all-to-all(bf16[128,8,128]{2,1,0:T(8,128)(2,1)S(1)} %broadcast_in_dim.45), channel_id=1, replica_groups=mesh['user_outer'=8,'core'=2,'party'=16] {'user_outer','party'}, dimensions={0} | all-to-all | bytes 524288 | tf_op jit(solution)/shard_map/all_to_all | solution.py:49
  155.6 2.8 collective-permute-start.3
  159.6 6.6 %fusion.5 = (f32[256,2048]{1,0:T(8,128)}, f32[256,2048]{1,0:T(8,128)}, f32[256,2048]{1,0:T(8,128)S(1)}) fusion(bf16[256,2048]{1,0:T(8,128)(2,1)S(1)} %bitcast.88, f32[]{:T(128)} %bitcast.17, f32[256,2048]{1,0:T(8,128)} %get-tuple-element.15, bf16[1024,2048]{1,0:T(8,128)(2,1)} %param.12, bf16[512,256]{1,0:T(8,128)(2,1)S(1)} %get-tuple-element.11, ...), kind=kOutput, calls=%fused_computation.12 | convolution fusion | flops 1078984704 | bytes 14155780 | tf_op jit(solution)/shard_map/dot_general | solution.py:115
  166.2 1.2 fusion.7
  167.5 1.4 broadcast_in_dim.46
  168.8 5.3 %all-to-all-start.5 = ((f32[256,1,128]{2,1,0:T(1,128)}), f32[256,1,128]{2,1,0:T(1,128)S(1)}, u32[]{:S(2)}, u32[]{:S(2)}) async-start(f32[256,1,128]{2,1,0:T(1,128)} %broadcast_in_dim.46), calls=%async_computation.5 | async-start | bytes 262144 | tf_op jit(solution)/shard_map/all_to_all | solution.py:58
  174.1 142.7 %all-reduce.2.cloned.1.call-done = f32[64,256]{1,0:T(8,128)} async-done(((f32[64,256]{1,0:T(8,128)}), f32[64,256]{1,0:T(8,128)}) %all-reduce.2.cloned.1.call-update) | async-done | bytes 65552 | tf_op jit(solution)/shard_map/psum | solution.py:95
  316.9 1.5 convert_subtract_fusion.2
  318.4 4.2 %shard_map.86 = (f32[2048,256]{1,0:T(8,128)}, f32[2048,256]{1,0:T(8,128)}) custom-call(f32[1]{0:T(128)} %bitcast.16.scale_ref, bf16[2048,256]{1,0:T(8,128)(2,1)} %w_ref.1, f32[256,2048]{1,0:T(8,128)} %get-tuple-element.9.first_ref, f32[256,2048]{1,0:T(8,128)} %get-tuple-element.8.last_ref), custom_call_target="tpu_custom_call" | custom-call | tf_op jit(solution)/shard_map/pallas_call | solution.py:72
  322.8 3.8 %multiply_subtract_fusion = f32[2048,256]{1,0:T(8,128)} fusion(f32[2048,256]{1,0:T(8,128)} %get-tuple-element.4, f32[2048,256]{1,0:T(8,128)} %get-tuple-element.5, f32[]{:T(128)} %bitcast.33), kind=kLoop, calls=%fused_computation.16 | loop fusion | flops 1048576 | bytes 6291460 | tf_op jit(solution)/shard_map/sub | solution.py:129
  (36 shorter events, 7.6 us)
Async XLA Ops:
  7.2 1.1 copy-start
  7.2 4.8 %copy-start.2 = (bf16[2048,256]{1,0:T(8,128)(2,1)S(1)}, bf16[2048,256]{1,0:T(8,128)(2,1)}, u32[]{:S(2)}) copy-start(bf16[2048,256]{1,0:T(8,128)(2,1)} %w_ref.1) | copy-start | bytes 3145732
  10.8 5.0 %copy-start.6 = (f32[64,256]{1,0:T(8,128)}, f32[64,256]{1,0:T(8,128)S(1)}, u32[]{:S(2)}) copy-start(f32[64,256]{1,0:T(8,128)S(1)} %fusion.13) | copy-start | bytes 196612
  11.9 3.9 %copy-start.3 = (f32[1024,256]{1,0:T(8,128)}, f32[1024,256]{1,0:T(8,128)S(1)}, u32[]{:S(2)}) copy-start(f32[1024,256]{1,0:T(8,128)S(1)} %scatter_custom_fusion) | copy-start | bytes 3145732
  11.9 304.9 %all-reduce.2.cloned.1.call-start = ((), (), s32[]{:S(2)}) async-start(), calls=%async_computation.6 | async-start | bytes 131072 | tf_op jit(solution)/shard_map/psum | solution.py:95
  15.8 1.0 copy-start.5
  16.8 4.8 %collective-permute-start = (f32[512,256]{1,0:T(8,128)S(1)}, f32[512,256]{1,0:T(8,128)S(1)}, u32[]{:S(2)}, u32[]{:S(2)}) collective-permute-start(f32[512,256]{1,0:T(8,128)S(1)} %dynamic-slice_bitcast_fusion.1), channel_id=1, source_target_pairs={{0,16},{16,0},{1,17},{17,1},{2,18},{18,2},{3,19},{19,3},{4,20},{20... | collective-permute-start | bytes 1572872 | tf_op jit(solution)/shard_map/ppermute | solution.py:32
  75.0 4.3 %collective-permute-start.1 = (bf16[512,256]{1,0:T(8,128)(2,1)S(1)}, bf16[512,256]{1,0:T(8,128)(2,1)S(1)}, u32[]{:S(2)}, u32[]{:S(2)}) collective-permute-start(bf16[512,256]{1,0:T(8,128)(2,1)S(1)} %bitcast.98), channel_id=1, source_target_pairs={{0,16},{16,0},{1,17},{17,1},{2,18},{18,2},{3,19},{19,3},{4,20},{20... | collective-permute-start | bytes 786440 | tf_op jit(solution)/shard_map/ppermute | solution.py:32
  79.3 24.5 %copy-start.4 = (f32[1024,256]{1,0:T(8,128)S(1)}, f32[1024,256]{1,0:T(8,128)}, u32[]{:S(2)}) copy-start(f32[1024,256]{1,0:T(8,128)} %copy-done.3) | copy-start | bytes 3145732
  108.1 2.8 collective-permute-start.2
  155.6 3.9 %collective-permute-start.3 = (bf16[512,256]{1,0:T(8,128)(2,1)S(1)}, bf16[512,256]{1,0:T(8,128)(2,1)S(1)}, u32[]{:S(2)}, u32[]{:S(2)}) collective-permute-start(bf16[512,256]{1,0:T(8,128)(2,1)S(1)} %bitcast.96), channel_id=1, source_target_pairs={{0,16},{16,0},{1,17},{17,1},{2,18},{18,2},{3,19},{19,3},{4,20},{20... | collective-permute-start | bytes 786440 | tf_op jit(solution)/shard_map/ppermute | solution.py:32
  159.6 6.6 %copy-start.1 = (f32[256,2048]{1,0:T(8,128)S(1)}, f32[256,2048]{1,0:T(8,128)}, u32[]{:S(2)}) copy-start(f32[256,2048]{1,0:T(8,128)} %get-tuple-element.15) | copy-start | bytes 6291460
  168.8 153.8 %all-to-all-start.5 = ((f32[256,1,128]{2,1,0:T(1,128)}), f32[256,1,128]{2,1,0:T(1,128)S(1)}, u32[]{:S(2)}, u32[]{:S(2)}) async-start(f32[256,1,128]{2,1,0:T(1,128)} %broadcast_in_dim.46), calls=%async_computation.5 | async-start | bytes 262144 | tf_op jit(solution)/shard_map/all_to_all | solution.py:58
Sparse Core Ops, SparseCore 0:
  158.5 158.2 all-reduce.1
